TPU v7x, 32 devices: a whole 2x2x4 slice. The times are simulated.
32 devices in a mesh: groups: 2 (over y), cent: 4 (over z), dp: 2 (over x), sub: 2 (over core).
Axes of the slice: x: 2, y: 2, z: 4, core: 2. Of those that a mesh axis runs over, the one named last changes fastest.
Arguments:
- embeddings: bfloat16 [1024, 768], P(('groups', 'cent', 'dp', 'sub')), parts along dimension 0, may hold values from -6 to 6
- weights: int32 [1024], P(('groups', 'cent', 'dp', 'sub')), parts along dimension 0, may hold values from 1 to 4
- centroids: bfloat16 [16384, 768], P(('groups', 'cent')), parts along dimension 0, may hold values from -6 to 6
- inverse_temp: float32 [1], replicated, may hold values from 16 to 256
Outputs:
- centroid_sums: float32 [16384, 768], P(('groups', 'cent', 'dp', 'sub')), parts along dimension 0
- renormed: bfloat16 [16384, 768], P(('groups', 'cent', 'dp', 'sub')), parts along dimension 0
- objective: float32 [1024], P(('groups', 'cent', 'dp', 'sub')), parts along dimension 0
There are 2 independent parts, one for each index of `groups`. A program takes and returns all parts, laid end to end along the dimension named above; an argument that names none is the same for every part. Nothing has to cross between parts.
All inputs are finite; a program needn't handle non-finite values.
Results may differ from a plain program's by a relative error of at most 0.0075.
The roundings to bfloat16 on the way count: a program that leaves them out, or rounds other values in their place, can miss the bound.
Values may be sent and summed in bfloat16 or wider, within the bound.
No kernel may reach another device: no remote copies, remote signals or barrier semaphores. Data moves between devices by JAX's collectives and lax.ppermute only.
A program may use at most 64 MiB of HBM per device.

v0:
```python
import jax
import jax.numpy as jnp
from jax import lax
from jax.sharding import PartitionSpec as P


def normalize(values):
    floats = values.astype(jnp.float32)
    return floats * lax.rsqrt(jnp.sum(floats * floats, axis=-1, keepdims=True) + 1e-06)


def shards(embeddings, weights, centroids, inverse_temp):
    sharpness = inverse_temp[0]
    unit_rows = normalize(embeddings).astype(jnp.bfloat16)
    unit_panel = normalize(centroids).astype(jnp.bfloat16)
    gathered_rows, gathered_weights = (
        lax.all_gather(unit_rows, "cent", axis=0, tiled=True),
        lax.all_gather(weights, "cent", axis=0, tiled=True),
    )
    scores = (
        lax.dot_general(
            gathered_rows, unit_panel, (((1,), (1,)), ((), ())), preferred_element_type=jnp.float32
        )
        * sharpness
    )
    local_peak = jnp.max(scores, axis=1)
    row_peak = lax.pmax(local_peak, "cent")
    row_total = lax.psum(jnp.sum(jnp.exp(scores - row_peak[:, None]), axis=1), "cent")
    log_sum = row_peak + jnp.log(row_total)
    weight_float = gathered_weights.astype(jnp.float32)
    responsibility = (weight_float[:, None] * jnp.exp(scores - log_sum[:, None])).astype(
        jnp.bfloat16
    )
    partial_value = lax.dot_general(
        responsibility, gathered_rows, (((0,), (0,)), ((), ())), preferred_element_type=jnp.float32
    ).astype(jnp.bfloat16)
    ones_row = jnp.ones((1, responsibility.shape[0]), jnp.bfloat16)
    weight_mass = jnp.dot(ones_row, responsibility, preferred_element_type=jnp.float32)[0].astype(
        jnp.bfloat16
    )
    own_count = centroids.shape[0] // lax.axis_size(("dp", "sub"))
    offset = lax.axis_index(("dp", "sub")) * own_count
    panel_sums, panel_mass = (
        lax.psum(partial_value, ("dp", "sub")).astype(jnp.float32),
        lax.psum(weight_mass, ("dp", "sub")).astype(jnp.float32),
    )
    centroid_sums = lax.dynamic_slice_in_dim(panel_sums, offset, own_count, 0)
    own_mass = lax.dynamic_slice_in_dim(panel_mass, offset, own_count, 0)
    own_cents = lax.dynamic_slice_in_dim(unit_panel, offset, own_count, 0).astype(jnp.float32)
    moved = own_cents + centroid_sums / (own_mass + 1.0)[:, None]
    renormed = normalize(moved).astype(jnp.bfloat16)
    row_offset = lax.axis_index("cent") * embeddings.shape[0]
    weighted_log_sum = weight_float * log_sum / sharpness
    objective = lax.dynamic_slice_in_dim(weighted_log_sum, row_offset, embeddings.shape[0], 0)
    return (centroid_sums, renormed, objective)


def solution(mesh):
    in_specs = (
        P(("groups", "cent", "dp", "sub"), None),
        P(("groups", "cent", "dp", "sub")),
        P(("groups", "cent"), None),
        P(),
    )
    out_specs = (
        P(("groups", "cent", "dp", "sub"), None),
        P(("groups", "cent", "dp", "sub"), None),
        P(("groups", "cent", "dp", "sub")),
    )
    return jax.shard_map(shards, mesh=mesh, in_specs=in_specs, out_specs=out_specs, check_vma=False)
```

profile of v0, /device:TPU:0, one launch (start us, length us, event | category | flops | bytes accessed | tf_op | source)
XLA Modules:
  0.0 144.0 jit_solution(1710212666322466163)
XLA Ops:
  7.2 0.0 copy-start.3
  7.2 0.0 all-reduce.3.cloned.1.call-start
  7.9 0.9 fusion.2
  8.8 1.2 dynamic-slice
  10.7 0.9 dynamic-update-slice
  11.6 9.9 %all-reduce = s32[128]{0:T(128)S(1)} all-reduce(s32[128]{0:T(128)S(1)} %dynamic-update-slice), channel_id=1, replica_groups=mesh['groups'=2,'cent'=4,'dp'=2,'sub'=2] {'cent'}, use_global_device_ids=true, to_apply=%add | all-reduce | flops 128 | bytes 1024
  21.5 0.0 copy-start
  21.5 2.7 %fusion = f32[2048]{0:T(1024)S(1)} fusion(bf16[2048,768]{1,0:T(8,128)(2,1)} %param.6), kind=kLoop, calls=%fused_computation.2 | loop fusion | flops 4716544 | bytes 3153920 | tf_op jit(solution)/shard_map/reduce_sum | solution.py:9
  24.2 0.0 copy-done.3
  24.2 0.1 fusion.3
  24.3 13.6 %all_gather.7 = bf16[128,768]{1,0:T(8,128)(2,1)S(1)} all-gather(bf16[32,768]{1,0:T(8,128)(2,1)S(1)} %fusion.3), channel_id=1, replica_groups=mesh['groups'=2,'cent'=4,'dp'=2,'sub'=2] {'cent'}, dimensions={0}, use_global_device_ids=true | all-gather | bytes 245760 | tf_op jit(solution)/shard_map/all_gather | solution.py:17
  37.9 0.0 copy-done
  37.9 0.6 fusion.1
  38.4 2.1 %fusion.7 = (f32[128]{0:T(128)S(1)}, f32[128,2048]{1,0:T(8,128)}) fusion(f32[]{:T(128)} %bitcast.8, bf16[128,768]{1,0:T(8,128)(2,1)S(1)} %all_gather.7, bf16[2048,768]{1,0:T(8,128)(2,1)S(1)} %fusion.1), kind=kOutput, calls=%fused_computation.25 | convolution fusion | flops 403177344 | bytes 4391428 | tf_op jit(solution)/shard_map/dot_general | solution.py:21
  40.6 10.4 %pmax.7 = f32[128]{0:T(128)S(1)} all-reduce(f32[128]{0:T(128)S(1)} %get-tuple-element.7), channel_id=1, replica_groups=mesh['groups'=2,'cent'=4,'dp'=2,'sub'=2] {'cent'}, use_global_device_ids=true, to_apply=%region_3.0 | all-reduce | flops 128 | bytes 1024 | tf_op jit(solution)/shard_map/pmax | solution.py:27
  51.0 1.5 %exponential_reduce_fusion = f32[128]{0:T(128)S(1)} fusion(f32[128,2048]{1,0:T(8,128)} %get-tuple-element.8, f32[128]{0:T(128)S(1)} %pmax.7), kind=kLoop, calls=%fused_computation.10 | loop fusion | flops 524160 | bytes 1049600 | tf_op jit(solution)/shard_map/reduce_sum | solution.py:28
  52.5 8.4 %psum.21 = f32[128]{0:T(128)S(1)} all-reduce(f32[128]{0:T(128)S(1)} %exponential_reduce_fusion), channel_id=1, replica_groups=mesh['groups'=2,'cent'=4,'dp'=2,'sub'=2] {'cent'}, use_global_device_ids=true, to_apply=%region_5.0 | all-reduce | flops 128 | bytes 1024 | tf_op jit(solution)/shard_map/psum | solution.py:28
  60.9 1.5 %multiply_convert_fusion.1 = bf16[128,2048]{1,0:T(8,128)(2,1)S(1)} fusion(f32[128,2048]{1,0:T(8,128)} %get-tuple-element.8, f32[128]{0:T(128)S(1)} %get-tuple-element.4, f32[128]{0:T(128)S(1)} %convert_element_type.36), kind=kLoop, calls=%fused_computation.9 | loop fusion | flops 786432 | bytes 1573888 | tf_op jit(solution)/shard_map/convert_element_type | solution.py:31
  62.4 0.0 copy-start.2
  62.4 0.8 copy-done.2
  63.2 2.7 %convolution_convert_fusion = bf16[2048,768]{1,0:T(8,128)(2,1)} fusion(bf16[128,2048]{1,0:T(8,128)(2,1)S(1)} %multiply_convert_fusion.1, bf16[128,768]{1,0:T(8,128)(2,1)S(1)} %all_gather.7), kind=kOutput, calls=%fused_computation.4 | convolution fusion | flops 404226048 | bytes 3866624 | tf_op jit(solution)/shard_map/dot_general | solution.py:34
  65.9 0.0 all-reduce.3.cloned.1.call-update
  65.9 1.2 fusion.4
  67.2 0.6 dynamic_slice.15
  67.7 5.6 %psum.23 = bf16[2048]{0:T(1024)(128)(2,1)S(1)} all-reduce(bf16[2048]{0:T(1024)(128)(2,1)S(1)} %convert_element_type.45), channel_id=1, replica_groups=mesh['groups'=2,'cent'=4,'dp'=2,'sub'=2] {'dp','sub'}, use_global_device_ids=true, to_apply=%region_7.0 | all-reduce | flops 2048 | bytes 8192 | tf_op jit(solution)/shard_map/psum | solution.py:45
  73.4 0.1 convert_add_fusion
  73.5 60.7 %all-reduce.3.cloned.1.call-done = bf16[2048,768]{1,0:T(8,128)(2,1)} async-done(((bf16[2048,768]{1,0:T(8,128)(2,1)}), bf16[2048,768]{1,0:T(8,128)(2,1)}) %all-reduce.3.cloned.1.call-update) | async-done | bytes 3145744 | tf_op jit(solution)/shard_map/psum | solution.py:44
  134.2 1.6 %multiply_reduce_fusion = (f32[512]{0:T(512)S(1)}, f32[512,768]{1,0:T(8,128)S(1)}) fusion(f32[512]{0:T(512)S(1)} %convert_add_fusion, bf16[2048,768]{1,0:T(8,128)(2,1)S(1)} %fusion.1, s32[]{:T(128)S(6)} %select_n.8, bf16[2048,768]{1,0:T(8,128)(2,1)} %all-reduce.3.cloned.1.call-done), kind=kLoop, calls=%fused_computation.7 | loop fusion | flops 2358784 | bytes 3149828 | tf_op jit(solution)/shard_map/reduce_sum | solution.py:9
  135.8 0.0 copy-start.1
  135.8 1.4 multiply_convert_fusion
  137.2 0.0 copy-done.1
  (7 shorter events, 0.0 us)
Async XLA Ops:
  7.2 17.0 %copy-start.3 = (bf16[32,768]{1,0:T(8,128)(2,1)S(1)}, bf16[32,768]{1,0:T(8,128)(2,1)}, u32[]{:S(2)}) copy-start(bf16[32,768]{1,0:T(8,128)(2,1)} %param.4) | copy-start | bytes 147460
  7.2 127.0 %all-reduce.3.cloned.1.call-start = ((), (), s32[]{:S(2)}) async-start(), calls=%async_computation | async-start | bytes 6291456 | tf_op jit(solution)/shard_map/psum | solution.py:44
  21.5 16.4 %copy-start = (bf16[2048,768]{1,0:T(8,128)(2,1)S(1)}, bf16[2048,768]{1,0:T(8,128)(2,1)}, u32[]{:S(2)}) copy-start(bf16[2048,768]{1,0:T(8,128)(2,1)} %param.6) | copy-start | bytes 9437188
  62.4 0.8 copy-start.2
  135.8 1.4 copy-start.1
Sparse Core Ops, SparseCore 0:
  66.0 68.1 all-reduce.2
where the time goes:
time: 145 us; the launch traced here: 144 us
  waiting for transfers between devices  60.8 us (42%)
  blocking collectives  47.9 us (33%)
  between operations  15.4 us (11%)
  other arithmetic  10.4 us (7%)
  matrix products  6.06 us (4%)
  local copies, waits for them, and re-layouts  3.49 us (2%)
    psum x1, waiting for transfers between devices, shards(): lax.psum(partial_value, ('dp', 'sub')).astype(jnp.float32)  60.7 us
    all_gather x1, blocking collectives, shards(): lax.all_gather(unit_rows, 'cent', axis=0, tiled=True)  13.6 us
    pmax x1, blocking collectives, shards(): row_peak = lax.pmax(local_peak, 'cent')  10.4 us
    unnamed x1, blocking collectives  9.89 us
    psum x1, blocking collectives, shards(): lax.psum(jnp.sum(jnp.exp(scores - row_peak[:, None]), axis=1), 'cent')  8.37 us
    psum x1, blocking collectives, shards(): lax.psum(weight_mass, ('dp', 'sub')).astype(jnp.float32)  5.64 us
    reduce_sum x3, other arithmetic, normalize(): jnp.sum(floats * floats, axis=-1, keepdims=True) + 1e-06  5.22 us
    unnamed x11, local copies, waits for them, and re-layouts  2.9 us
  transfers between devices with their start and end apart: 1, of which 1 were waited for; matrix products, arithmetic and copies ran while one was open for 1% of the time, Pallas kernels for 0%

commit v1 on v0

--- a/solution.py
+++ b/solution.py
@@ -2,6 +2,28 @@
 import jax.numpy as jnp
 from jax import lax
 from jax.sharding import PartitionSpec as P
+
+
+def in_order(parts, dim):
+    shape = list(parts.shape[1:])
+    shape[dim] *= parts.shape[0]
+    return jnp.moveaxis(parts, 0, dim).reshape(shape)
+
+
+def gather_around(x, axis, dim):
+    peers = lax.axis_size(axis)
+    pairs = [(i, (i + 1) % peers) for i in range(peers)]
+    back = [(b, a) for a, b in pairs]
+    lower, upper = ([], [])
+    for step in range(peers - 1):
+        if step % 2 == 0:
+            lower.append(lax.ppermute(lower[-1] if lower else x, axis, pairs))
+        else:
+            upper.append(lax.ppermute(upper[-1] if upper else x, axis, back))
+    tiles = jnp.stack([*lower[::-1], x, *upper])
+    shift = lax.axis_index(axis) - len(lower)
+    tiles = tiles[(jnp.arange(peers) - shift) % peers]
+    return in_order(tiles, dim)
 
 
 def normalize(values):
@@ -14,7 +36,7 @@
     unit_rows = normalize(embeddings).astype(jnp.bfloat16)
     unit_panel = normalize(centroids).astype(jnp.bfloat16)
     gathered_rows, gathered_weights = (
-        lax.all_gather(unit_rows, "cent", axis=0, tiled=True),
+        gather_around(unit_rows, "cent", 0),
         lax.all_gather(weights, "cent", axis=0, tiled=True),
     )
     scores = (

time: 145 us -> 137 us (0.945)
  blocking collectives: 47.9 us -> 33.1 us
  starting transfers between devices: 0.04 us -> 5.1 us
  other arithmetic: 10.4 us -> 12.1 us
    all_gather x1 -> x0, blocking collectives: 13.6 us -> none  [shards(): lax.all_gather(unit_rows, 'cent', axis=0, tiled=True)]
    ppermute x0 -> x3, starting transfers between devices: none -> 5.06 us  [the longest x1 5.05 us: gather_around(): upper.append(lax.ppermute(upper[-1] if upper else x, axis, back))]
    ppermute x0 -> x3, waiting for transfers between devices: none -> 1.58 us  [the longest x2 1.57 us: gather_around(): lower.append(lax.ppermute(lower[-1] if lower else x, axis, pairs))]
    unnamed x11 -> x13, local copies, waits for them, and re-layouts: 2.9 us -> 1.72 us
  transfers between devices with their start and end apart: 1 -> 4, of which waited for: 1 -> 2; matrix products, arithmetic and copies ran while one was open for 1% -> 5% of each run, Pallas kernels for 0% -> 0%
where the time goes in v1:
time: 137 us
  waiting for transfers between devices  61.9 us (45%)
  blocking collectives  33.1 us (24%)
  between operations  15.5 us (11%)
  other arithmetic  12.1 us (9%)
  matrix products  6.06 us (4%)
  starting transfers between devices  5.1 us (4%)
  local copies, waits for them, and re-layouts  2.86 us (2%)
    psum x1, waiting for transfers between devices, shards(): lax.psum(partial_value, ('dp', 'sub')).astype(jnp.float32)  60.3 us
    pmax x1, blocking collectives, shards(): row_peak = lax.pmax(local_peak, 'cent')  9.84 us
    psum x1, blocking collectives, shards(): lax.psum(jnp.sum(jnp.exp(scores - row_peak[:, None]), axis=1), 'cent')  8.87 us
    unnamed x1, blocking collectives  8.72 us
    psum x1, blocking collectives, shards(): lax.psum(weight_mass, ('dp', 'sub')).astype(jnp.float32)  5.64 us
    reduce_sum x3, other arithmetic, normalize(): jnp.sum(floats * floats, axis=-1, keepdims=True) + 1e-06  5.22 us
    ppermute x1, starting transfers between devices, gather_around(): upper.append(lax.ppermute(upper[-1] if upper else x, axis, back))  5.05 us
  transfers between devices with their start and end apart: 4, of which 2 were waited for; matrix products, arithmetic and copies ran while one was open for 5% of the time, Pallas kernels for 0%

profile of v1, /device:TPU:0, one launch (start us, length us, event | category | flops | bytes accessed | tf_op | source)
XLA Modules:
  0.0 136.5 jit_solution(15673804480127829627)
XLA Ops:
  7.2 0.0 all-reduce.3.cloned.1.call-start
  7.2 0.9 fusion.2
  8.1 0.9 fusion.3
  9.0 5.1 %collective-permute-start.2 = (bf16[32,768]{1,0:T(8,128)(2,1)S(1)}, bf16[32,768]{1,0:T(8,128)(2,1)S(1)}, u32[]{:S(2)}, u32[]{:S(2)}) collective-permute-start(bf16[32,768]{1,0:T(8,128)(2,1)S(1)} %fusion.3), channel_id=1, source_target_pairs={{4,0},{8,4},{12,8},{0,12},{5,1},{9,5},{13,9},{1,13},{6,2},{10,6},{... | collective-permute-start | bytes 147464 | tf_op jit(solution)/shard_map/ppermute | solution.py:22
  14.1 0.0 collective-permute-start
  14.1 0.9 fusion.15
  14.9 0.0 copy-start
  15.0 2.7 %fusion = f32[2048]{0:T(1024)S(1)} fusion(bf16[2048,768]{1,0:T(8,128)(2,1)} %param.6), kind=kLoop, calls=%fused_computation.3 | loop fusion | flops 4716544 | bytes 3153920 | tf_op jit(solution)/shard_map/reduce_sum | solution.py:31
  17.7 0.1 copy-done
  17.8 0.0 copy-start.4
  17.8 0.0 copy-start.3
  17.8 0.6 fusion.1
  18.4 1.6 %collective-permute-done = bf16[32,768]{1,0:T(8,128)(2,1)S(1)} collective-permute-done((bf16[32,768]{1,0:T(8,128)(2,1)S(1)}, bf16[32,768]{1,0:T(8,128)(2,1)S(1)}, u32[]{:S(2)}, u32[]{:S(2)}) %collective-permute-start) | collective-permute-done | bytes 49184 | tf_op jit(solution)/shard_map/ppermute | solution.py:20
  20.0 0.0 collective-permute-start.1
  20.6 0.0 copy-done.4
  20.6 0.6 dynamic-slice
  21.9 0.0 copy-done.3
  21.9 0.2 dynamic-update-slice
  22.1 8.7 %all-reduce = s32[128]{0:T(128)S(1)} all-reduce(s32[128]{0:T(128)S(1)} %dynamic-update-slice), channel_id=1, replica_groups=mesh['groups'=2,'cent'=4,'dp'=2,'sub'=2] {'cent'}, use_global_device_ids=true, to_apply=%add | all-reduce | flops 128 | bytes 1024
  30.9 0.0 collective-permute-done.2
  30.9 0.0 collective-permute-done.1
  30.9 0.6 gather_fusion
  31.5 2.1 %fusion.9 = (f32[128]{0:T(128)S(1)}, f32[128,2048]{1,0:T(8,128)}) fusion(f32[]{:T(128)} %bitcast.16, bf16[128,768]{1,0:T(8,128)(2,1)S(1)} %bitcast.18, bf16[2048,768]{1,0:T(8,128)(2,1)S(1)} %fusion.1), kind=kOutput, calls=%fused_computation.34 | convolution fusion | flops 403177344 | bytes 4391428 | tf_op jit(solution)/shard_map/dot_general | solution.py:43
  33.6 9.8 %pmax.7 = f32[128]{0:T(128)S(1)} all-reduce(f32[128]{0:T(128)S(1)} %get-tuple-element.7), channel_id=1, replica_groups=mesh['groups'=2,'cent'=4,'dp'=2,'sub'=2] {'cent'}, use_global_device_ids=true, to_apply=%region_3.4 | all-reduce | flops 128 | bytes 1024 | tf_op jit(solution)/shard_map/pmax | solution.py:49
  43.4 1.5 %exponential_reduce_fusion = f32[128]{0:T(128)S(1)} fusion(f32[128,2048]{1,0:T(8,128)} %get-tuple-element.8, f32[128]{0:T(128)S(1)} %pmax.7), kind=kLoop, calls=%fused_computation.11 | loop fusion | flops 524160 | bytes 1049600 | tf_op jit(solution)/shard_map/reduce_sum | solution.py:50
  45.0 8.9 %psum.21 = f32[128]{0:T(128)S(1)} all-reduce(f32[128]{0:T(128)S(1)} %exponential_reduce_fusion), channel_id=1, replica_groups=mesh['groups'=2,'cent'=4,'dp'=2,'sub'=2] {'cent'}, use_global_device_ids=true, to_apply=%region_5.6 | all-reduce | flops 128 | bytes 1024 | tf_op jit(solution)/shard_map/psum | solution.py:50
  53.8 1.5 %multiply_convert_fusion.1 = bf16[128,2048]{1,0:T(8,128)(2,1)S(1)} fusion(f32[128,2048]{1,0:T(8,128)} %get-tuple-element.8, f32[128]{0:T(128)S(1)} %get-tuple-element.4, f32[128]{0:T(128)S(1)} %convert_element_type.36), kind=kLoop, calls=%fused_computation.10 | loop fusion | flops 786432 | bytes 1573888 | tf_op jit(solution)/shard_map/convert_element_type | solution.py:53
  55.3 0.0 copy-start.2
  55.4 0.8 copy-done.2
  56.1 2.7 %convolution_convert_fusion = bf16[2048,768]{1,0:T(8,128)(2,1)} fusion(bf16[128,2048]{1,0:T(8,128)(2,1)S(1)} %multiply_convert_fusion.1, bf16[128,768]{1,0:T(8,128)(2,1)S(1)} %bitcast.19), kind=kOutput, calls=%fused_computation.5 | convolution fusion | flops 404226048 | bytes 3866624 | tf_op jit(solution)/shard_map/dot_general | solution.py:56
  58.9 0.0 all-reduce.3.cloned.1.call-update
  58.9 1.2 fusion.6
  60.1 0.6 dynamic_slice.15
  60.7 5.6 %psum.23 = bf16[2048]{0:T(1024)(128)(2,1)S(1)} all-reduce(bf16[2048]{0:T(1024)(128)(2,1)S(1)} %convert_element_type.45), channel_id=1, replica_groups=mesh['groups'=2,'cent'=4,'dp'=2,'sub'=2] {'dp','sub'}, use_global_device_ids=true, to_apply=%region_7.8 | all-reduce | flops 2048 | bytes 8192 | tf_op jit(solution)/shard_map/psum | solution.py:67
  66.3 0.1 convert_add_fusion
  66.4 60.3 %all-reduce.3.cloned.1.call-done = bf16[2048,768]{1,0:T(8,128)(2,1)} async-done(((bf16[2048,768]{1,0:T(8,128)(2,1)}), bf16[2048,768]{1,0:T(8,128)(2,1)}) %all-reduce.3.cloned.1.call-update) | async-done | bytes 3145744 | tf_op jit(solution)/shard_map/psum | solution.py:66
  126.7 1.6 %multiply_reduce_fusion = (f32[512]{0:T(512)S(1)}, f32[512,768]{1,0:T(8,128)S(1)}) fusion(f32[512]{0:T(512)S(1)} %convert_add_fusion, bf16[2048,768]{1,0:T(8,128)(2,1)S(1)} %fusion.1, s32[]{:T(128)S(6)} %select_n.34, bf16[2048,768]{1,0:T(8,128)(2,1)} %all-reduce.3.cloned.1.call-done), kind=kLoop, calls=%fused_computation.8 | loop fusion | flops 2358784 | bytes 3149828 | tf_op jit(solution)/shard_map/reduce_sum | solution.py:31
  128.3 0.0 copy-start.1
  128.3 1.4 %multiply_convert_fusion = bf16[512,768]{1,0:T(8,128)(2,1)} fusion(f32[512]{0:T(512)S(1)} %add_rsqrt_fusion.1, f32[512,768]{1,0:T(8,128)S(1)} %get-tuple-element.6, f32[512]{0:T(512)S(1)} %convert_add_fusion, bf16[2048,768]{1,0:T(8,128)(2,1)S(1)} %fusion.1, s32[]{:T(128)S(6)} %select_n.34), kind=kLoop, calls=%fused_computation.7 | loop fusion | flops 1966080 | bytes 3149828 | tf_op jit(solution)/shard_map/convert_element_type | solution.py:73
  129.7 0.0 copy-done.1
  (10 shorter events, 0.1 us)
Async XLA Ops:
  7.2 119.5 %all-reduce.3.cloned.1.call-start = ((), (), s32[]{:S(2)}) async-start(), calls=%async_computation | async-start | bytes 6291456 | tf_op jit(solution)/shard_map/psum | solution.py:66
  9.0 21.8 %collective-permute-start.2 = (bf16[32,768]{1,0:T(8,128)(2,1)S(1)}, bf16[32,768]{1,0:T(8,128)(2,1)S(1)}, u32[]{:S(2)}, u32[]{:S(2)}) collective-permute-start(bf16[32,768]{1,0:T(8,128)(2,1)S(1)} %fusion.3), channel_id=1, source_target_pairs={{4,0},{8,4},{12,8},{0,12},{5,1},{9,5},{13,9},{1,13},{6,2},{10,6},{... | collective-permute-start | bytes 147464 | tf_op jit(solution)/shard_map/ppermute | solution.py:22
  14.1 5.9 %collective-permute-start = (bf16[32,768]{1,0:T(8,128)(2,1)S(1)}, bf16[32,768]{1,0:T(8,128)(2,1)S(1)}, u32[]{:S(2)}, u32[]{:S(2)}) collective-permute-start(bf16[32,768]{1,0:T(8,128)(2,1)S(1)} %fusion.3), channel_id=1, source_target_pairs={{0,4},{4,8},{8,12},{12,0},{1,5},{5,9},{9,13},{13,1},{2,6},{6,10},{... | collective-permute-start | bytes 147464 | tf_op jit(solution)/shard_map/ppermute | solution.py:20
  14.9 2.8 %copy-start = (bf16[2048,768]{1,0:T(8,128)(2,1)S(1)}, bf16[2048,768]{1,0:T(8,128)(2,1)}, u32[]{:S(2)}) copy-start(bf16[2048,768]{1,0:T(8,128)(2,1)} %param.6) | copy-start | bytes 9437188
  17.8 2.8 %copy-start.4 = (u32[32]{0:T(128)S(1)}, u32[32]{0:T(128)}, u32[]{:S(2)}) copy-start(u32[32]{0:T(128)} %constant.55) | copy-start | bytes 388
  17.8 4.1 %copy-start.3 = (s32[32]{0:T(128)S(1)}, s32[32]{0:T(128)}, u32[]{:S(2)}) copy-start(s32[32]{0:T(128)} %param.5) | copy-start | bytes 388
  20.0 10.9 %collective-permute-start.1 = (bf16[32,768]{1,0:T(8,128)(2,1)S(1)}, bf16[32,768]{1,0:T(8,128)(2,1)S(1)}, u32[]{:S(2)}, u32[]{:S(2)}) collective-permute-start(bf16[32,768]{1,0:T(8,128)(2,1)S(1)} %collective-permute-done), channel_id=1, source_target_pairs={{0,4},{4,8},{8,12},{12,0},{1,5},{5,9},{9,13},{13,1},{2,6},{6,10},{... | collective-permute-start | bytes 147464 | tf_op jit(solution)/shard_map/ppermute | solution.py:20
  55.3 0.8 copy-start.2
  128.3 1.4 %copy-start.1 = (f32[512,768]{1,0:T(8,128)}, f32[512,768]{1,0:T(8,128)S(1)}, u32[]{:S(2)}) copy-start(f32[512,768]{1,0:T(8,128)S(1)} %get-tuple-element.6) | copy-start | bytes 4718596
Sparse Core Ops, SparseCore 0:
  59.0 67.6 all-reduce.2
